TPU v7x, 256 devices: a whole 4x4x8 slice. The times are simulated.
256 devices in a mesh: row: 16 (over x, z_lo), col: 16 (over y, z_hi, core).
Axes of the slice: x: 4, y: 4, z: 8 (z_hi: 2, z_lo: 4; z = z_hi * 4 + z_lo), core: 2. Of those that a mesh axis runs over, the one named last changes fastest.
Arguments:
- hidden: bfloat16 [2560, 8192], P('row', 'col'), may hold values from -6 to 6
- w_query: bfloat16 [8192, 8192], P('col', 'row'), may hold values from -0.0625 to 0.0625
- w_keyval: bfloat16 [8192, 2048], P('col', 'row'), may hold values from -0.15625 to 0.15625
- prefix_cache: bfloat16 [2, 16384, 2048], P(None, 'col', 'row'), may hold values from -60 to 60, as said below
- suffix_lengths: int32 [16], replicated, may hold values from 32 to 160, as said below
- group_ids: int32 [16], replicated, may hold values from 0 to 1, as said below
Outputs:
- attended: bfloat16 [2560, 8192], P('col', 'row')
Inputs may be any that keep to these rules, and one draw needn't show every extreme that they name: `suffix_lengths`: every suffix has 32 to 160 live tokens; some request has exactly 160 and some exactly 32. `group_ids`: exactly 8 requests read each prefix. `prefix_cache`: finite values.
All inputs are finite; a program needn't handle non-finite values.
Results may differ from a plain program's by a relative error of at most 0.011.
Values may be sent and summed in bfloat16 or wider, within the bound.
No kernel may reach another device: no remote copies, remote signals or barrier semaphores. Data moves between devices by JAX's collectives and lax.ppermute only.
A program may use at most 128 MiB of HBM per device.

v0:
```python
import jax
import jax.numpy as jnp
from jax import lax
from jax.sharding import PartitionSpec as P

HD = 128
PREFIX = 16384
SUF = 160


def partner(value, axis, stride):
    mask = 2**stride
    pairs = [(source, source ^ mask) for source in range(lax.axis_size(axis))]
    return lax.ppermute(value, axis, pairs)


def rotary_tables(positions):
    freqs = 500000.0 ** (-(jnp.arange(HD // 2, dtype=jnp.float32) * 2.0 / HD))
    angles = positions.astype(jnp.float32)[:, None] * freqs[None, :]
    return (jnp.cos(angles), jnp.sin(angles))


def rotate(values, cosine, sine):
    first = values[..., : HD // 2]
    second = values[..., HD // 2 :]
    cosine = cosine[:, None, :]
    sine = sine[:, None, :]
    return jnp.concatenate(
        [first * cosine - second * sine, second * cosine + first * sine], axis=-1
    )


def block_size(count):
    size = count
    for _ in range(24):
        if size > 2048 and size % 2 == 0:
            size = size // 2
    return size


def block_stats(req_query, keys, values, scale):
    scores = jnp.einsum("thd,kd->htk", req_query, keys, preferred_element_type=jnp.float32) * scale
    top = jnp.max(scores, axis=-1)
    weights = jnp.exp(scores - top[..., None])
    total = jnp.sum(weights, axis=-1)
    accum = jnp.einsum(
        "htk,kd->htd", weights.astype(jnp.bfloat16), values, preferred_element_type=jnp.float32
    )
    return (top, total, accum)


def combine(first, second):
    top = jnp.maximum(first[0], second[0])
    scale_one = jnp.exp(first[0] - top)
    scale_two = jnp.exp(second[0] - top)
    total = first[1] * scale_one + second[1] * scale_two
    accum = first[2] * scale_one[..., None] + second[2] * scale_two[..., None]
    return (top, total, accum)


def empty_state(heads_here):
    return (
        jnp.full((heads_here, SUF), -1e30, jnp.float32),
        jnp.zeros((heads_here, SUF), jnp.float32),
        jnp.zeros((heads_here, SUF, HD), jnp.float32),
    )


def attend_keys(req_query, keys, values, scale):
    count = keys.shape[0]
    size = block_size(count)
    key_blocks = keys.reshape(count // size, size, HD)
    value_blocks = values.reshape(count // size, size, HD)

    def advance(state, pieces):
        return (combine(state, block_stats(req_query, pieces[0], pieces[1], scale)), None)

    state, _ = lax.scan(advance, empty_state(req_query.shape[1]), (key_blocks, value_blocks))
    return state


def flat_perm(n_row, n_col, target):
    pairs = []
    for r in range(n_row):
        for c in range(n_col):
            dest = target(r, c)
            if dest is not None:
                pairs.append((r * n_col + c, dest[0] * n_col + dest[1]))
    return pairs


def combine_all(states):
    top = states[0][0]
    for state in states[1:]:
        top = jnp.maximum(top, state[0])
    total = 0.0
    accum = 0.0
    for state in states:
        factor = jnp.exp(state[0] - top)
        total = total + state[1] * factor
        accum = accum + state[2] * factor[..., None]
    return (top, total, accum)


def per_device(hidden, w_query, w_keyval, prefix_cache, suffix_lengths, group_ids):
    n_row = lax.axis_size("row")
    n_col = lax.axis_size("col")
    row_id = lax.axis_index("row")
    col_id = lax.axis_index("col")
    heads_here = w_query.shape[1] // HD
    segments = w_keyval.shape[1] // HD
    scale = 1.0 / HD**0.5
    gathered = lax.all_gather(hidden, "row", axis=0, tiled=True)
    weights_all = jnp.concatenate([w_query, w_keyval], axis=1)
    tok_block = gathered.shape[0] // n_col
    projected = lax.psum_scatter(
        jnp.dot(gathered, weights_all, preferred_element_type=jnp.float32),
        "col",
        scatter_dimension=0,
        tiled=True,
    )
    positions = PREFIX + jnp.arange(tok_block, dtype=jnp.int32) % SUF
    cosine, sine = rotary_tables(positions)
    query = projected[:, : heads_here * HD].reshape(tok_block, heads_here, HD)
    query = rotate(query, cosine, sine).astype(jnp.bfloat16)
    keyval = projected[:, heads_here * HD :].reshape(tok_block, segments, HD)
    segment_ids = row_id * segments + jnp.arange(segments, dtype=jnp.int32)
    is_key = segment_ids % 2 == 0
    keyval = jnp.where(is_key[None, :, None], rotate(keyval, cosine, sine), keyval).astype(
        jnp.bfloat16
    )
    odd = row_id % 2
    is_even = odd == 0
    other_keyval, other_cache = partner((keyval, prefix_cache), "row", 0)
    suffix_keys = jnp.where(is_even, keyval[:, 0], other_keyval[:, 0])
    suffix_values = jnp.where(is_even, other_keyval[:, 0], keyval[:, 0])
    cache_keys = jnp.where(is_even, prefix_cache, other_cache)
    cache_values = jnp.where(is_even, other_cache, prefix_cache)
    kv_block = jnp.concatenate([cache_keys, cache_values], axis=-1)
    half_bit = 2
    handled = col_id ^ half_bit * odd
    masks = [m for m in range(1, n_col) if m & half_bit == 0]
    blocks = [lax.dynamic_index_in_dim(kv_block, group_ids[handled], 0, keepdims=False)]
    for mask in masks:
        peer_group = group_ids[col_id ^ mask ^ half_bit * odd]
        piece = lax.dynamic_index_in_dim(kv_block, peer_group, 0, keepdims=False)
        pairs = [(c, c ^ mask) for c in range(n_col)]
        blocks.append(lax.ppermute(piece, "col", pairs))
    half_kv = jnp.concatenate(blocks, axis=0)
    half_keys = half_kv[:, :HD]
    half_values = half_kv[:, HD:]
    axes = ("row", "col")
    cross = flat_perm(
        n_row, n_col, lambda r, c: (r ^ 1, c ^ half_bit) if r % 2 == 0 else (r ^ 1, c)
    )
    back = flat_perm(n_row, n_col, lambda r, c: (r ^ 1, c) if r % 2 == 0 else (r ^ 1, c ^ half_bit))
    same = flat_perm(n_row, n_col, lambda r, c: (r, c ^ half_bit) if r % 2 == 1 else None)
    q_cross = lax.ppermute(query, axes, cross)
    q_same = lax.ppermute(query, axes, same)
    q_first = jnp.where(is_even, query, q_cross)
    q_second = jnp.where(is_even, q_cross, q_same)
    q_all = jnp.concatenate([q_first, q_second], axis=1)
    half_state = attend_keys(q_all, half_keys, half_values, scale)
    mine = jax.tree.map(
        lambda a, b: jnp.where(is_even, a, b),
        jax.tree.map(lambda x: x[:heads_here], half_state),
        jax.tree.map(lambda x: x[heads_here:], half_state),
    )
    theirs = jax.tree.map(
        lambda a, b: jnp.where(is_even, a, b),
        jax.tree.map(lambda x: x[heads_here:], half_state),
        jax.tree.map(lambda x: x[:heads_here], half_state),
    )
    from_cross = lax.ppermute(theirs, axes, back)
    from_same = lax.ppermute(mine, axes, same)
    first_state = jax.tree.map(lambda a, b: jnp.where(is_even, a, b), mine, from_same)
    length = suffix_lengths[col_id]
    places = jnp.arange(SUF, dtype=jnp.int32)
    mask = (places[None, :] <= places[:, None]) & (places[None, :] < length)
    scores = (
        jnp.einsum("thd,kd->htk", query, suffix_keys, preferred_element_type=jnp.float32) * scale
    )
    scores = jnp.where(mask[None], scores, -1e30)
    own_top = jnp.max(scores, axis=-1)
    weights = jnp.exp(scores - own_top[..., None])
    own_total = jnp.sum(weights, axis=-1)
    own_accum = jnp.einsum(
        "htk,kd->htd",
        weights.astype(jnp.bfloat16),
        suffix_values,
        preferred_element_type=jnp.float32,
    )
    merged = combine_all([first_state, from_cross, (own_top, own_total, own_accum)])
    result = merged[2] / merged[1][..., None]
    live = (places < length).astype(jnp.float32)
    result = result * live[None, :, None]
    return jnp.transpose(result, (1, 0, 2)).reshape(tok_block, heads_here * HD).astype(jnp.bfloat16)


def solution(mesh):
    return jax.shard_map(
        per_device,
        mesh=mesh,
        in_specs=(
            P("row", "col"),
            P("col", "row"),
            P("col", "row"),
            P(None, "col", "row"),
            P(),
            P(),
        ),
        out_specs=P("col", "row"),
        check_vma=False,
    )
```

profile of v0, /device:TPU:32, one launch (start us, length us, event | category | flops | bytes accessed | tf_op | source)
XLA Modules:
  0.0 354.4 jit_solution(18435070876985730292)
XLA Ops:
  7.3 91.1 %all-gather.2.cloned.1.call-done = bf16[2560,512]{1,0:T(8,128)(2,1)} async-done(((bf16[160,512]{1,0:T(8,128)(2,1)}), bf16[2560,512]{1,0:T(8,128)(2,1)}) %all-gather.2.cloned.1.call-update) | async-done | bytes 2621456 | tf_op jit(solution)/shard_map/all_gather | solution.py:113
  98.4 6.6 %convolution_bitcast_fusion = f32[2560,640]{0,1:T(8,128)} fusion(bf16[2560,512]{1,0:T(8,128)(2,1)} %all-gather.2.cloned.1.call-done, bf16[512,128]{1,0:T(8,128)(2,1)} %param.10, bf16[512,512]{1,0:T(8,128)(2,1)} %param.9), kind=kOutput, calls=%fused_computation.22 | convolution fusion | flops 1679032320 | bytes 9830400 | tf_op jit(solution)/shard_map/dot_general | solution.py:117
  105.0 8.1 %copy.37 = f32[2560,640]{1,0:T(8,128)} copy(f32[2560,640]{0,1:T(8,128)} %convolution_bitcast_fusion) | data formatting | bytes 13107200
  139.3 3.7 %collective-permute-start.4 = (bf16[1024,256]{1,0:T(8,128)(2,1)S(1)}, bf16[1024,256]{1,0:T(8,128)(2,1)S(1)}, u32[]{:S(2)}, u32[]{:S(2)}) collective-permute-start(bf16[1024,256]{1,0:T(8,128)(2,1)S(1)} %get-tuple-element.101), channel_id=1, source_target_pairs={{0,8},{1,9},{2,10},{3,11},{4,12},{5,13},{6,14},{7,15},{8,0},{9,1},... | collective-permute-start | bytes 1572872 | tf_op jit(solution)/shard_map/ppermute | solution.py:148
  149.7 11.7 %collective-permute-done.3 = bf16[1024,256]{1,0:T(8,128)(2,1)} collective-permute-done((bf16[1024,256]{1,0:T(8,128)(2,1)}, bf16[1024,256]{1,0:T(8,128)(2,1)}, u32[]{:S(2)}, u32[]{:S(2)}) %collective-permute-start.3) | collective-permute-done | bytes 524320 | tf_op jit(solution)/shard_map/ppermute | solution.py:148
  162.5 14.7 %collective-permute-done.4 = bf16[1024,256]{1,0:T(8,128)(2,1)S(1)} collective-permute-done((bf16[1024,256]{1,0:T(8,128)(2,1)S(1)}, bf16[1024,256]{1,0:T(8,128)(2,1)S(1)}, u32[]{:S(2)}, u32[]{:S(2)}) %collective-permute-start.4) | collective-permute-done | bytes 524320 | tf_op jit(solution)/shard_map/ppermute | solution.py:148
  177.2 11.4 %collective-permute-done.5 = bf16[1024,256]{1,0:T(8,128)(2,1)S(1)} collective-permute-done((bf16[1024,256]{1,0:T(8,128)(2,1)S(1)}, bf16[1024,256]{1,0:T(8,128)(2,1)S(1)}, u32[]{:S(2)}, u32[]{:S(2)}) %collective-permute-start.5) | collective-permute-done | bytes 524320 | tf_op jit(solution)/shard_map/ppermute | solution.py:148
  188.7 14.9 %collective-permute-done.7 = bf16[1024,256]{1,0:T(8,128)(2,1)S(1)} collective-permute-done((bf16[1024,256]{1,0:T(8,128)(2,1)S(1)}, bf16[1024,256]{1,0:T(8,128)(2,1)S(1)}, u32[]{:S(2)}, u32[]{:S(2)}) %collective-permute-start.7) | collective-permute-done | bytes 524320 | tf_op jit(solution)/shard_map/ppermute | solution.py:148
  205.2 32.0 %reduce-scatter.4.cloned.1.call-done = f32[160,640]{1,0:T(8,128)} async-done(((f32[2560,640]{1,0:T(8,128)}), f32[160,640]{1,0:T(8,128)}) %reduce-scatter.4.cloned.1.call-update) | async-done | bytes 409616
  254.4 12.5 %collective-permute-done.8 = bf16[160,4,128]{2,0,1:T(8,128)(2,1)S(1)} collective-permute-done((bf16[160,4,128]{2,0,1:T(8,128)(2,1)S(1)}, bf16[160,4,128]{2,0,1:T(8,128)(2,1)S(1)}, u32[]{:S(2)}, u32[]{:S(2)}) %collective-permute-start.8) | collective-permute-done | bytes 163872 | tf_op jit(solution)/shard_map/ppermute | solution.py:158
  267.0 55.0 %while.15 = (s32[]{:T(128)}, f32[8,160]{1,0:T(8,128)S(1)}, f32[8,160]{1,0:T(8,128)S(1)}, f32[8,160,128]{2,1,0:T(8,128)S(1)}, bf16[4,2048,128]{2,1,0:T(8,128)(2,1...) while((s32[]{:T(128)}, f32[8,160]{1,0:T(8,128)S(1)}, ...), condition=%wide.region_4.5_spmd.clone, body=%wide.region_1.4_spmd.clone.sunk | while | flops 1363811840 | bytes 76168840 | solution.py:78
  267.0 2.7 bitcast_reduce_fusion.2
  269.7 4.0 %copy-done = f32[2048,160,8]{0,1,2:T(8,128)} copy-done((f32[2048,160,8]{0,1,2:T(8,128)}, f32[2048,160,8]{0,1,2:T(8,128)S(1)}, u32[]{:S(2)}) %copy-start) | copy-done | bytes 10485784 | tf_op jit(solution)/shard_map/while
  275.6 5.1 %fusion.85 = f32[8,160,128]{2,1,0:T(8,128)S(1)} fusion(f32[2048,160,8]{0,1,2:T(8,128)} %copy-done, f32[8,160]{1,0:T(8,128)S(1)} %get-tuple-element.181, f32[8,160,128]{2,1,0:T(8,128)S(1)} %get-tuple-element.198, bf16[4,2048,128]{2,1,0:T(8,128)(2,1)S(1)} %get-tuple-element.210, s32[]{:T(128)} %get-tuple-element.195, ...), kind=kOutput, calls=%fused_computation.7.clone.1 | convolution fusion | flops 679608320 | bytes 12345349 | tf_op jit(solution)/shard_map/while/body/eval_jaxpr/htk,kd->htd/dot_general | solution.py:46
  283.5 4.0 %copy-done = f32[2048,160,8]{0,1,2:T(8,128)} copy-done((f32[2048,160,8]{0,1,2:T(8,128)}, f32[2048,160,8]{0,1,2:T(8,128)S(1)}, u32[]{:S(2)}) %copy-start) | copy-done | bytes 10485784 | tf_op jit(solution)/shard_map/while
  289.4 5.1 %fusion.85 = f32[8,160,128]{2,1,0:T(8,128)S(1)} fusion(f32[2048,160,8]{0,1,2:T(8,128)} %copy-done, f32[8,160]{1,0:T(8,128)S(1)} %get-tuple-element.181, f32[8,160,128]{2,1,0:T(8,128)S(1)} %get-tuple-element.198, bf16[4,2048,128]{2,1,0:T(8,128)(2,1)S(1)} %get-tuple-element.210, s32[]{:T(128)} %get-tuple-element.195, ...), kind=kOutput, calls=%fused_computation.7.clone.1 | convolution fusion | flops 679608320 | bytes 12345349 | tf_op jit(solution)/shard_map/while/body/eval_jaxpr/htk,kd->htd/dot_general | solution.py:46
  297.2 4.0 %copy-done = f32[2048,160,8]{0,1,2:T(8,128)} copy-done((f32[2048,160,8]{0,1,2:T(8,128)}, f32[2048,160,8]{0,1,2:T(8,128)S(1)}, u32[]{:S(2)}) %copy-start) | copy-done | bytes 10485784 | tf_op jit(solution)/shard_map/while
  303.2 5.1 %fusion.85 = f32[8,160,128]{2,1,0:T(8,128)S(1)} fusion(f32[2048,160,8]{0,1,2:T(8,128)} %copy-done, f32[8,160]{1,0:T(8,128)S(1)} %get-tuple-element.181, f32[8,160,128]{2,1,0:T(8,128)S(1)} %get-tuple-element.198, bf16[4,2048,128]{2,1,0:T(8,128)(2,1)S(1)} %get-tuple-element.210, s32[]{:T(128)} %get-tuple-element.195, ...), kind=kOutput, calls=%fused_computation.7.clone.1 | convolution fusion | flops 679608320 | bytes 12345349 | tf_op jit(solution)/shard_map/while/body/eval_jaxpr/htk,kd->htd/dot_general | solution.py:46
  311.0 4.0 %copy-done = f32[2048,160,8]{0,1,2:T(8,128)} copy-done((f32[2048,160,8]{0,1,2:T(8,128)}, f32[2048,160,8]{0,1,2:T(8,128)S(1)}, u32[]{:S(2)}) %copy-start) | copy-done | bytes 10485784 | tf_op jit(solution)/shard_map/while
  316.9 5.1 %fusion.85 = f32[8,160,128]{2,1,0:T(8,128)S(1)} fusion(f32[2048,160,8]{0,1,2:T(8,128)} %copy-done, f32[8,160]{1,0:T(8,128)S(1)} %get-tuple-element.181, f32[8,160,128]{2,1,0:T(8,128)S(1)} %get-tuple-element.198, bf16[4,2048,128]{2,1,0:T(8,128)(2,1)S(1)} %get-tuple-element.210, s32[]{:T(128)} %get-tuple-element.195, ...), kind=kOutput, calls=%fused_computation.7.clone.1 | convolution fusion | flops 679608320 | bytes 12345349 | tf_op jit(solution)/shard_map/while/body/eval_jaxpr/htk,kd->htd/dot_general | solution.py:46
  322.1 3.8 %collective-permute-start.10 = (f32[4,160,128]{2,1,0:T(8,128)S(1)}, f32[4,160,128]{2,1,0:T(8,128)S(1)}, u32[]{:S(2)}, u32[]{:S(2)}) collective-permute-start(f32[4,160,128]{2,1,0:T(8,128)S(1)} %get-tuple-element.107), channel_id=1, source_target_pairs={{16,18},{17,19},{18,16},{19,17},{20,22},{21,23},{22,20},{23,21},{2... | collective-permute-start | bytes 983048 | tf_op jit(solution)/shard_map/ppermute | solution.py:175
  326.0 6.0 %collective-permute-start.11 = (f32[4,160]{1,0:T(4,128)S(1)}, f32[4,160]{1,0:T(4,128)S(1)}, u32[]{:S(2)}, u32[]{:S(2)}) collective-permute-start(f32[4,160]{1,0:T(4,128)S(1)} %get-tuple-element.115), channel_id=1, source_target_pairs={{16,18},{17,19},{18,16},{19,17},{20,22},{21,23},{22,20},{23,21},{2... | collective-permute-start | bytes 7688 | tf_op jit(solution)/shard_map/ppermute | solution.py:175
  332.1 3.8 %collective-permute-start.15 = (f32[4,160]{1,0:T(4,128)S(1)}, f32[4,160]{1,0:T(4,128)S(1)}, u32[]{:S(2)}, u32[]{:S(2)}) collective-permute-start(f32[4,160]{1,0:T(4,128)S(1)} %get-tuple-element.117), channel_id=1, source_target_pairs={{16,18},{17,19},{18,16},{19,17},{20,22},{21,23},{22,20},{23,21},{2... | collective-permute-start | bytes 7688 | tf_op jit(solution)/shard_map/ppermute | solution.py:175
  335.9 5.6 %collective-permute-done.11 = f32[4,160]{1,0:T(4,128)S(1)} collective-permute-done((f32[4,160]{1,0:T(4,128)S(1)}, f32[4,160]{1,0:T(4,128)S(1)}, u32[]{:S(2)}, u32[]{:S(2)}) %collective-permute-start.11) | collective-permute-done | bytes 2592 | tf_op jit(solution)/shard_map/ppermute | solution.py:175
  (103 shorter events, 59.7 us)
Async XLA Ops:
  6.5 91.9 %all-gather.2.cloned.1.call-start = ((), (), s32[]{:S(2)}) async-start(), calls=%async_computation.1 | async-start | bytes 2785280 | tf_op jit(solution)/shard_map/all_gather | solution.py:113
  7.3 230.0 %reduce-scatter.4.cloned.1.call-start = ((), (), s32[]{:S(2)}) async-start(), calls=%async_computation.2 | async-start | bytes 6963200
  113.2 14.9 %copy-start.7 = (s32[16]{0:T(128)S(1)}, s32[16]{0:T(128)}, u32[]{:S(2)}) copy-start(s32[16]{0:T(128)} %param.12) | copy-start | bytes 196
  114.2 16.2 %collective-permute-start = (bf16[2,1024,128]{2,1,0:T(8,128)(2,1)S(1)}, bf16[2,1024,128]{2,1,0:T(8,128)(2,1)S(1)}, u32[]{:S(2)}, u32[]{:S(2)}) collective-permute-start(bf16[2,1024,128]{2,1,0:T(8,128)(2,1)S(1)} %copy-done.1), channel_id=1, source_target_pairs={{0,16},{16,0},{32,48},{48,32},{64,80},{80,64},{96,112},{112,96},{1... | collective-permute-start | bytes 1572872 | tf_op jit(solution)/shard_map/ppermute | solution.py:14
  128.7 8.8 %copy-start.6 = (f32[64]{0:T(128)}, f32[64]{0:T(128)S(1)}, u32[]{:S(2)}) copy-start(f32[64]{0:T(128)S(1)} %negate_power_fusion) | copy-start | bytes 772
  131.9 11.4 %collective-permute-start.1 = (bf16[1024,256]{1,0:T(8,128)(2,1)}, bf16[1024,256]{1,0:T(8,128)(2,1)}, u32[]{:S(2)}, u32[]{:S(2)}) collective-permute-start(bf16[1024,256]{1,0:T(8,128)(2,1)} %get-tuple-element.98), channel_id=1, source_target_pairs={{0,1},{1,0},{2,3},{3,2},{4,5},{5,4},{6,7},{7,6},{8,9},{9,8},{10,11... | collective-permute-start | bytes 1572872 | tf_op jit(solution)/shard_map/ppermute | solution.py:148
  131.9 15.1 %collective-permute-start.2 = (bf16[1024,256]{1,0:T(8,128)(2,1)}, bf16[1024,256]{1,0:T(8,128)(2,1)}, u32[]{:S(2)}, u32[]{:S(2)}) collective-permute-start(bf16[1024,256]{1,0:T(8,128)(2,1)} %get-tuple-element.99), channel_id=1, source_target_pairs={{0,4},{1,5},{2,6},{3,7},{4,0},{5,1},{6,2},{7,3},{8,12},{9,13},{10,... | collective-permute-start | bytes 1572872 | tf_op jit(solution)/shard_map/ppermute | solution.py:148
  134.2 27.2 %collective-permute-start.3 = (bf16[1024,256]{1,0:T(8,128)(2,1)}, bf16[1024,256]{1,0:T(8,128)(2,1)}, u32[]{:S(2)}, u32[]{:S(2)}) collective-permute-start(bf16[1024,256]{1,0:T(8,128)(2,1)} %get-tuple-element.100), channel_id=1, source_target_pairs={{0,5},{1,4},{2,7},{3,6},{4,1},{5,0},{6,3},{7,2},{8,13},{9,12},{10,... | collective-permute-start | bytes 1572872 | tf_op jit(solution)/shard_map/ppermute | solution.py:148
  139.3 37.9 %collective-permute-start.4 = (bf16[1024,256]{1,0:T(8,128)(2,1)S(1)}, bf16[1024,256]{1,0:T(8,128)(2,1)S(1)}, u32[]{:S(2)}, u32[]{:S(2)}) collective-permute-start(bf16[1024,256]{1,0:T(8,128)(2,1)S(1)} %get-tuple-element.101), channel_id=1, source_target_pairs={{0,8},{1,9},{2,10},{3,11},{4,12},{5,13},{6,14},{7,15},{8,0},{9,1},... | collective-permute-start | bytes 1572872 | tf_op jit(solution)/shard_map/ppermute | solution.py:148
  143.1 45.5 %collective-permute-start.5 = (bf16[1024,256]{1,0:T(8,128)(2,1)S(1)}, bf16[1024,256]{1,0:T(8,128)(2,1)S(1)}, u32[]{:S(2)}, u32[]{:S(2)}) collective-permute-start(bf16[1024,256]{1,0:T(8,128)(2,1)S(1)} %get-tuple-element.102), channel_id=1, source_target_pairs={{0,9},{1,8},{2,11},{3,10},{4,13},{5,12},{6,15},{7,14},{8,1},{9,0},... | collective-permute-start | bytes 1572872 | tf_op jit(solution)/shard_map/ppermute | solution.py:148
  143.2 45.4 %collective-permute-start.6 = (bf16[1024,256]{1,0:T(8,128)(2,1)S(1)}, bf16[1024,256]{1,0:T(8,128)(2,1)S(1)}, u32[]{:S(2)}, u32[]{:S(2)}) collective-permute-start(bf16[1024,256]{1,0:T(8,128)(2,1)S(1)} %fusion.43), channel_id=1, source_target_pairs={{0,12},{1,13},{2,14},{3,15},{4,8},{5,9},{6,10},{7,11},{8,4},{9,5},... | collective-permute-start | bytes 1572872 | tf_op jit(solution)/shard_map/ppermute | solution.py:148
  147.0 56.6 %collective-permute-start.7 = (bf16[1024,256]{1,0:T(8,128)(2,1)S(1)}, bf16[1024,256]{1,0:T(8,128)(2,1)S(1)}, u32[]{:S(2)}, u32[]{:S(2)}) collective-permute-start(bf16[1024,256]{1,0:T(8,128)(2,1)S(1)} %get-tuple-element.97), channel_id=1, source_target_pairs={{0,13},{1,12},{2,15},{3,14},{4,9},{5,8},{6,11},{7,10},{8,5},{9,4},... | collective-permute-start | bytes 1572872 | tf_op jit(solution)/shard_map/ppermute | solution.py:148
  245.7 21.3 %copy-start.2 = (bf16[160,128]{0,1:T(8,128)(2,1)}, bf16[160,128]{0,1:T(8,128)(2,1)S(1)}, u32[]{:S(2)}) copy-start(bf16[160,128]{0,1:T(8,128)(2,1)S(1)} %fusion.52) | copy-start | bytes 122884
  245.7 6.7 %collective-permute-start.13 = (bf16[160,1,128]{0,2,1:T(8,128)(2,1)S(1)}, bf16[160,1,128]{0,2,1:T(8,128)(2,1)S(1)}, u32[]{:S(2)}, u32[]{:S(2)}) collective-permute-start(bf16[160,1,128]{0,2,1:T(8,128)(2,1)S(1)} %bitcast.113), channel_id=1, source_target_pairs={{0,16},{16,0},{32,48},{48,32},{64,80},{80,64},{96,112},{112,96},{1... | collective-permute-start | bytes 122888 | tf_op jit(solution)/shard_map/ppermute | solution.py:14
  249.3 17.6 %collective-permute-start.8 = (bf16[160,4,128]{2,0,1:T(8,128)(2,1)S(1)}, bf16[160,4,128]{2,0,1:T(8,128)(2,1)S(1)}, u32[]{:S(2)}, u32[]{:S(2)}) collective-permute-start(bf16[160,4,128]{2,0,1:T(8,128)(2,1)S(1)} %pad_maximum_fusion.1), channel_id=1, source_target_pairs={{0,18},{1,19},{2,16},{3,17},{4,22},{5,23},{6,20},{7,21},{8,26},{9,... | collective-permute-start | bytes 491528 | tf_op jit(solution)/shard_map/ppermute | solution.py:158
  249.4 17.5 %collective-permute-start.9 = (bf16[160,4,128]{2,0,1:T(8,128)(2,1)S(1)}, bf16[160,4,128]{2,0,1:T(8,128)(2,1)S(1)}, u32[]{:S(2)}, u32[]{:S(2)}) collective-permute-start(bf16[160,4,128]{2,0,1:T(8,128)(2,1)S(1)} %pad_maximum_fusion.1), channel_id=1, source_target_pairs={{16,18},{17,19},{18,16},{19,17},{20,22},{21,23},{22,20},{23,21},{2... | collective-permute-start | bytes 491528 | tf_op jit(solution)/shard_map/ppermute | solution.py:159
  267.0 78.2 %copy-start.3 = (bf16[160,128]{0,1:T(8,128)(2,1)S(1)}, bf16[160,128]{0,1:T(8,128)(2,1)}, u32[]{:S(2)}) copy-start(bf16[160,128]{0,1:T(8,128)(2,1)} %copy-done.2) | copy-start | bytes 122884
  267.0 78.2 %copy-start.8 = (f32[160]{0:T(256)S(1)}, f32[160]{0:T(256)}, u32[]{:S(2)}) copy-start(f32[160]{0:T(256)} %fusion.66) | copy-start | bytes 1924
  322.1 23.0 %collective-permute-start.10 = (f32[4,160,128]{2,1,0:T(8,128)S(1)}, f32[4,160,128]{2,1,0:T(8,128)S(1)}, u32[]{:S(2)}, u32[]{:S(2)}) collective-permute-start(f32[4,160,128]{2,1,0:T(8,128)S(1)} %get-tuple-element.107), channel_id=1, source_target_pairs={{16,18},{17,19},{18,16},{19,17},{20,22},{21,23},{22,20},{23,21},{2... | collective-permute-start | bytes 983048 | tf_op jit(solution)/shard_map/ppermute | solution.py:175
  325.9 19.2 %collective-permute-start.14 = (f32[4,160,128]{2,1,0:T(8,128)S(1)}, f32[4,160,128]{2,1,0:T(8,128)S(1)}, u32[]{:S(2)}, u32[]{:S(2)}) collective-permute-start(f32[4,160,128]{2,1,0:T(8,128)S(1)} %get-tuple-element.108), channel_id=1, source_target_pairs={{0,16},{1,17},{2,18},{3,19},{4,20},{5,21},{6,22},{7,23},{8,24},{9,... | collective-permute-start | bytes 983048 | tf_op jit(solution)/shard_map/ppermute | solution.py:174
  326.0 15.5 %collective-permute-start.11 = (f32[4,160]{1,0:T(4,128)S(1)}, f32[4,160]{1,0:T(4,128)S(1)}, u32[]{:S(2)}, u32[]{:S(2)}) collective-permute-start(f32[4,160]{1,0:T(4,128)S(1)} %get-tuple-element.115), channel_id=1, source_target_pairs={{16,18},{17,19},{18,16},{19,17},{20,22},{21,23},{22,20},{23,21},{2... | collective-permute-start | bytes 7688 | tf_op jit(solution)/shard_map/ppermute | solution.py:175
  332.0 10.7 %collective-permute-start.12 = (f32[4,160]{1,0:T(4,128)S(1)}, f32[4,160]{1,0:T(4,128)S(1)}, u32[]{:S(2)}, u32[]{:S(2)}) collective-permute-start(f32[4,160]{1,0:T(4,128)S(1)} %get-tuple-element.116), channel_id=1, source_target_pairs={{0,16},{1,17},{2,18},{3,19},{4,20},{5,21},{6,22},{7,23},{8,24},{9,... | collective-permute-start | bytes 7688 | tf_op jit(solution)/shard_map/ppermute | solution.py:174
  332.1 10.6 %collective-permute-start.15 = (f32[4,160]{1,0:T(4,128)S(1)}, f32[4,160]{1,0:T(4,128)S(1)}, u32[]{:S(2)}, u32[]{:S(2)}) collective-permute-start(f32[4,160]{1,0:T(4,128)S(1)} %get-tuple-element.117), channel_id=1, source_target_pairs={{16,18},{17,19},{18,16},{19,17},{20,22},{21,23},{22,20},{23,21},{2... | collective-permute-start | bytes 7688 | tf_op jit(solution)/shard_map/ppermute | solution.py:175
  341.5 3.6 %collective-permute-start.16 = (f32[4,160]{1,0:T(4,128)S(1)}, f32[4,160]{1,0:T(4,128)S(1)}, u32[]{:S(2)}, u32[]{:S(2)}) collective-permute-start(f32[4,160]{1,0:T(4,128)S(1)} %get-tuple-element.118), channel_id=1, source_target_pairs={{0,16},{1,17},{2,18},{3,19},{4,20},{5,21},{6,22},{7,23},{8,24},{9,... | collective-permute-start | bytes 7688 | tf_op jit(solution)/shard_map/ppermute | solution.py:174
  (7 other events, 27.4 us)
Sparse Core Ops, SparseCore 0:
  9.1 89.2 all-gather.1
  113.3 123.8 reduce-scatter.3
where the time goes:
time: 356 us; the launch traced here: 354 us
  waiting for transfers between devices  198 us (56%)
  matrix products  41.5 us (12%)
  local copies, waits for them, and re-layouts  39.7 us (11%)
  starting transfers between devices  29.7 us (8%)
  between operations  29.4 us (8%)
  other arithmetic  16.2 us (5%)
    all_gather x1, waiting for transfers between devices, per_device(): gathered = lax.all_gather(hidden, 'row', axis=0, tiled=True)  91.1 us
    ppermute x7, waiting for transfers between devices, per_device(): blocks.append(lax.ppermute(piece, 'col', pairs))  52.8 us
    unnamed x3, waiting for transfers between devices  32.7 us
    dot_general x4, matrix products, block_stats(): jnp.einsum('htk,kd->htd', weights.astype(jnp.bfloat16), values, preferred...  20.6 us
    while x8, local copies, waits for them, and re-layouts  16.1 us
    unnamed x27, local copies, waits for them, and re-layouts  16 us
    ppermute x3, starting transfers between devices, per_device(): from_same = lax.ppermute(mine, axes, same)  13.5 us
    ppermute x1, waiting for transfers between devices, per_device(): q_cross = lax.ppermute(query, axes, cross)  12.5 us
  transfers between devices with their start and end apart: 19, of which 11 were waited for; matrix products, arithmetic and copies ran while one was open for 4% of the time, Pallas kernels for 0%

commit v1 on v0

--- a/solution.py
+++ b/solution.py
@@ -6,6 +6,14 @@
 HD = 128
 PREFIX = 16384
 SUF = 160
+
+
+def regions_render(patch, ax_name, array_axis):
+    local_part = jnp.concatenate(
+        jax.lax.all_to_all(jnp.stack([patch] * jax.lax.axis_size(ax_name), 0), ax_name, 0, 0),
+        array_axis,
+    )
+    return local_part
 
 
 def partner(value, axis, stride):
@@ -110,7 +118,7 @@
     heads_here = w_query.shape[1] // HD
     segments = w_keyval.shape[1] // HD
     scale = 1.0 / HD**0.5
-    gathered = lax.all_gather(hidden, "row", axis=0, tiled=True)
+    gathered = regions_render(hidden, "row", 0)
     weights_all = jnp.concatenate([w_query, w_keyval], axis=1)
     tok_block = gathered.shape[0] // n_col
     projected = lax.psum_scatter(

time: 356 us -> 331 us (0.930)
  waiting for transfers between devices: 198 us -> 106 us
  blocking collectives: 0 us -> 67.5 us
    all_gather x1 -> x0, waiting for transfers between devices: 91.1 us -> none  [per_device(): gathered = lax.all_gather(hidden, 'row', axis=0, tiled=True)]
    all_to_all x0 -> x1, blocking collectives: none -> 67.5 us  [regions_render(): jax.lax.all_to_all(jnp.stack([patch] * jax.lax.axis_size(ax_name), 0), ax...]
    unnamed x3 -> x2, waiting for transfers between devices: 32.7 us -> 31.6 us
    unnamed x27 -> x31, local copies, waits for them, and re-layouts: 16 us -> 16 us
  transfers between devices with their start and end apart: 19 -> 18, of which waited for: 11 -> 10; matrix products, arithmetic and copies ran while one was open for 4% -> 5% of each run, Pallas kernels for 0% -> 0%
where the time goes in v1:
time: 331 us; the launch traced here: 330 us
  waiting for transfers between devices  106 us (32%)
  blocking collectives  67.5 us (20%)
  local copies, waits for them, and re-layouts  40.8 us (12%)
  matrix products  39.5 us (12%)
  starting transfers between devices  31.1 us (9%)
  between operations  29 us (9%)
  other arithmetic  16.1 us (5%)
    all_to_all x1, blocking collectives, regions_render(): jax.lax.all_to_all(jnp.stack([patch] * jax.lax.axis_size(ax_name), 0), ax...  67.5 us
    ppermute x7, waiting for transfers between devices, per_device(): blocks.append(lax.ppermute(piece, 'col', pairs))  52.9 us
    unnamed x2, waiting for transfers between devices  31.6 us
    dot_general x4, matrix products, block_stats(): jnp.einsum('htk,kd->htd', weights.astype(jnp.bfloat16), values, preferred...  20.5 us
    while x8, local copies, waits for them, and re-layouts  16 us
    unnamed x31, local copies, waits for them, and re-layouts  16 us
    ppermute x3, starting transfers between devices, per_device(): from_same = lax.ppermute(mine, axes, same)  13.6 us
    ppermute x1, waiting for transfers between devices, per_device(): q_cross = lax.ppermute(query, axes, cross)  12.5 us
  transfers between devices with their start and end apart: 18, of which 10 were waited for; matrix products, arithmetic and copies ran while one was open for 5% of the time, Pallas kernels for 0%

profile of v1, /device:TPU:32, one launch (start us, length us, event | category | flops | bytes accessed | tf_op | source)
XLA Modules:
  0.0 330.0 jit_solution(7258325878981902189)
XLA Ops:
  7.8 67.5 %all_to_all.5 = bf16[16,160,512]{2,1,0:T(8,128)(2,1)S(1)} all-to-all(bf16[16,160,512]{2,1,0:T(8,128)(2,1)S(1)} %stack.2), channel_id=1, replica_groups=mesh['row'=16,'col'=16] {'row'}, dimensions={0} | all-to-all | bytes 5242880 | tf_op jit(solution)/shard_map/all_to_all | solution.py:13
  75.3 4.7 %convolution_bitcast_fusion = f32[2560,640]{0,1:T(8,128)} fusion(bf16[2560,512]{1,0:T(8,128)(2,1)S(1)} %bitcast.112, bf16[512,128]{1,0:T(8,128)(2,1)S(1)} %copy-done.8, bf16[512,512]{1,0:T(8,128)(2,1)S(1)} %copy-done.7), kind=kOutput, calls=%fused_computation.22 | convolution fusion | flops 1679032320 | bytes 9830400 | tf_op jit(solution)/shard_map/dot_general | solution.py:125
  80.0 8.1 %copy.37 = f32[2560,640]{1,0:T(8,128)} copy(f32[2560,640]{0,1:T(8,128)} %convolution_bitcast_fusion) | data formatting | bytes 13107200
  114.9 3.3 collective-permute-start.4
  118.4 3.0 collective-permute-start.6
  125.6 11.6 %collective-permute-done.3 = bf16[1024,256]{1,0:T(8,128)(2,1)} collective-permute-done((bf16[1024,256]{1,0:T(8,128)(2,1)}, bf16[1024,256]{1,0:T(8,128)(2,1)}, u32[]{:S(2)}, u32[]{:S(2)}) %collective-permute-start.3) | collective-permute-done | bytes 524320 | tf_op jit(solution)/shard_map/ppermute | solution.py:156
  138.2 14.8 %collective-permute-done.4 = bf16[1024,256]{1,0:T(8,128)(2,1)S(1)} collective-permute-done((bf16[1024,256]{1,0:T(8,128)(2,1)S(1)}, bf16[1024,256]{1,0:T(8,128)(2,1)S(1)}, u32[]{:S(2)}, u32[]{:S(2)}) %collective-permute-start.4) | collective-permute-done | bytes 524320 | tf_op jit(solution)/shard_map/ppermute | solution.py:156
  153.0 11.4 %collective-permute-done.5 = bf16[1024,256]{1,0:T(8,128)(2,1)S(1)} collective-permute-done((bf16[1024,256]{1,0:T(8,128)(2,1)S(1)}, bf16[1024,256]{1,0:T(8,128)(2,1)S(1)}, u32[]{:S(2)}, u32[]{:S(2)}) %collective-permute-start.5) | collective-permute-done | bytes 524320 | tf_op jit(solution)/shard_map/ppermute | solution.py:156
  164.5 15.0 %collective-permute-done.7 = bf16[1024,256]{1,0:T(8,128)(2,1)S(1)} collective-permute-done((bf16[1024,256]{1,0:T(8,128)(2,1)S(1)}, bf16[1024,256]{1,0:T(8,128)(2,1)S(1)}, u32[]{:S(2)}, u32[]{:S(2)}) %collective-permute-start.7) | collective-permute-done | bytes 524320 | tf_op jit(solution)/shard_map/ppermute | solution.py:156
  181.2 31.6 %reduce-scatter.4.cloned.1.call-done = f32[160,640]{1,0:T(8,128)} async-done(((f32[2560,640]{1,0:T(8,128)}), f32[160,640]{1,0:T(8,128)}) %reduce-scatter.4.cloned.1.call-update) | async-done | bytes 409616
  229.9 12.5 %collective-permute-done.8 = bf16[160,4,128]{2,0,1:T(8,128)(2,1)S(1)} collective-permute-done((bf16[160,4,128]{2,0,1:T(8,128)(2,1)S(1)}, bf16[160,4,128]{2,0,1:T(8,128)(2,1)S(1)}, u32[]{:S(2)}, u32[]{:S(2)}) %collective-permute-start.8) | collective-permute-done | bytes 163872 | tf_op jit(solution)/shard_map/ppermute | solution.py:166
  242.6 55.0 %while.15 = (s32[]{:T(128)}, f32[8,160]{1,0:T(8,128)S(1)}, f32[8,160]{1,0:T(8,128)S(1)}, f32[8,160,128]{2,1,0:T(8,128)S(1)}, bf16[4,2048,128]{2,1,0:T(8,128)(2,1...) while((s32[]{:T(128)}, f32[8,160]{1,0:T(8,128)S(1)}, ...), condition=%wide.region_4.5_spmd.clone, body=%wide.region_1.4_spmd.clone.sunk | while | flops 1363811840 | bytes 76168840 | solution.py:86
  245.2 4.0 %copy-done = f32[2048,160,8]{0,1,2:T(8,128)} copy-done((f32[2048,160,8]{0,1,2:T(8,128)}, f32[2048,160,8]{0,1,2:T(8,128)S(1)}, u32[]{:S(2)}) %copy-start) | copy-done | bytes 10485784 | tf_op jit(solution)/shard_map/while
  251.1 5.1 %fusion.85 = f32[8,160,128]{2,1,0:T(8,128)S(1)} fusion(f32[2048,160,8]{0,1,2:T(8,128)} %copy-done, f32[8,160]{1,0:T(8,128)S(1)} %get-tuple-element.181, f32[8,160,128]{2,1,0:T(8,128)S(1)} %get-tuple-element.198, bf16[4,2048,128]{2,1,0:T(8,128)(2,1)S(1)} %get-tuple-element.210, s32[]{:T(128)} %get-tuple-element.195, ...), kind=kOutput, calls=%fused_computation.7.clone.1 | convolution fusion | flops 679608320 | bytes 12345349 | tf_op jit(solution)/shard_map/while/body/eval_jaxpr/htk,kd->htd/dot_general | solution.py:54
  259.0 4.0 %copy-done = f32[2048,160,8]{0,1,2:T(8,128)} copy-done((f32[2048,160,8]{0,1,2:T(8,128)}, f32[2048,160,8]{0,1,2:T(8,128)S(1)}, u32[]{:S(2)}) %copy-start) | copy-done | bytes 10485784 | tf_op jit(solution)/shard_map/while
  264.9 5.1 %fusion.85 = f32[8,160,128]{2,1,0:T(8,128)S(1)} fusion(f32[2048,160,8]{0,1,2:T(8,128)} %copy-done, f32[8,160]{1,0:T(8,128)S(1)} %get-tuple-element.181, f32[8,160,128]{2,1,0:T(8,128)S(1)} %get-tuple-element.198, bf16[4,2048,128]{2,1,0:T(8,128)(2,1)S(1)} %get-tuple-element.210, s32[]{:T(128)} %get-tuple-element.195, ...), kind=kOutput, calls=%fused_computation.7.clone.1 | convolution fusion | flops 679608320 | bytes 12345349 | tf_op jit(solution)/shard_map/while/body/eval_jaxpr/htk,kd->htd/dot_general | solution.py:54
  272.7 4.0 %copy-done = f32[2048,160,8]{0,1,2:T(8,128)} copy-done((f32[2048,160,8]{0,1,2:T(8,128)}, f32[2048,160,8]{0,1,2:T(8,128)S(1)}, u32[]{:S(2)}) %copy-start) | copy-done | bytes 10485784 | tf_op jit(solution)/shard_map/while
  278.6 5.1 %fusion.85 = f32[8,160,128]{2,1,0:T(8,128)S(1)} fusion(f32[2048,160,8]{0,1,2:T(8,128)} %copy-done, f32[8,160]{1,0:T(8,128)S(1)} %get-tuple-element.181, f32[8,160,128]{2,1,0:T(8,128)S(1)} %get-tuple-element.198, bf16[4,2048,128]{2,1,0:T(8,128)(2,1)S(1)} %get-tuple-element.210, s32[]{:T(128)} %get-tuple-element.195, ...), kind=kOutput, calls=%fused_computation.7.clone.1 | convolution fusion | flops 679608320 | bytes 12345349 | tf_op jit(solution)/shard_map/while/body/eval_jaxpr/htk,kd->htd/dot_general | solution.py:54
  286.5 4.0 %copy-done = f32[2048,160,8]{0,1,2:T(8,128)} copy-done((f32[2048,160,8]{0,1,2:T(8,128)}, f32[2048,160,8]{0,1,2:T(8,128)S(1)}, u32[]{:S(2)}) %copy-start) | copy-done | bytes 10485784 | tf_op jit(solution)/shard_map/while
  292.4 5.1 %fusion.85 = f32[8,160,128]{2,1,0:T(8,128)S(1)} fusion(f32[2048,160,8]{0,1,2:T(8,128)} %copy-done, f32[8,160]{1,0:T(8,128)S(1)} %get-tuple-element.181, f32[8,160,128]{2,1,0:T(8,128)S(1)} %get-tuple-element.198, bf16[4,2048,128]{2,1,0:T(8,128)(2,1)S(1)} %get-tuple-element.210, s32[]{:T(128)} %get-tuple-element.195, ...), kind=kOutput, calls=%fused_computation.7.clone.1 | convolution fusion | flops 679608320 | bytes 12345349 | tf_op jit(solution)/shard_map/while/body/eval_jaxpr/htk,kd->htd/dot_general | solution.py:54
  297.6 3.8 %collective-permute-start.10 = (f32[4,160,128]{2,1,0:T(8,128)S(1)}, f32[4,160,128]{2,1,0:T(8,128)S(1)}, u32[]{:S(2)}, u32[]{:S(2)}) collective-permute-start(f32[4,160,128]{2,1,0:T(8,128)S(1)} %get-tuple-element.107), channel_id=1, source_target_pairs={{16,18},{17,19},{18,16},{19,17},{20,22},{21,23},{22,20},{23,21},{2... | collective-permute-start | bytes 983048 | tf_op jit(solution)/shard_map/ppermute | solution.py:183
  301.5 5.9 %collective-permute-start.11 = (f32[4,160]{1,0:T(4,128)S(1)}, f32[4,160]{1,0:T(4,128)S(1)}, u32[]{:S(2)}, u32[]{:S(2)}) collective-permute-start(f32[4,160]{1,0:T(4,128)S(1)} %get-tuple-element.115), channel_id=1, source_target_pairs={{16,18},{17,19},{18,16},{19,17},{20,22},{21,23},{22,20},{23,21},{2... | collective-permute-start | bytes 7688 | tf_op jit(solution)/shard_map/ppermute | solution.py:183
  307.6 3.8 %collective-permute-start.15 = (f32[4,160]{1,0:T(4,128)S(1)}, f32[4,160]{1,0:T(4,128)S(1)}, u32[]{:S(2)}, u32[]{:S(2)}) collective-permute-start(f32[4,160]{1,0:T(4,128)S(1)} %get-tuple-element.117), channel_id=1, source_target_pairs={{16,18},{17,19},{18,16},{19,17},{20,22},{21,23},{22,20},{23,21},{2... | collective-permute-start | bytes 7688 | tf_op jit(solution)/shard_map/ppermute | solution.py:183
  311.4 5.8 %collective-permute-done.11 = f32[4,160]{1,0:T(4,128)S(1)} collective-permute-done((f32[4,160]{1,0:T(4,128)S(1)}, f32[4,160]{1,0:T(4,128)S(1)}, u32[]{:S(2)}, u32[]{:S(2)}) %collective-permute-start.11) | collective-permute-done | bytes 2592 | tf_op jit(solution)/shard_map/ppermute | solution.py:183
  (106 shorter events, 61.5 us)
Async XLA Ops:
  6.5 68.8 %copy-start.8 = (bf16[512,128]{1,0:T(8,128)(2,1)S(1)}, bf16[512,128]{1,0:T(8,128)(2,1)}, u32[]{:S(2)}) copy-start(bf16[512,128]{1,0:T(8,128)(2,1)} %param.10) | copy-start | bytes 393220
  6.5 68.8 %copy-start.7 = (bf16[512,512]{1,0:T(8,128)(2,1)S(1)}, bf16[512,512]{1,0:T(8,128)(2,1)}, u32[]{:S(2)}) copy-start(bf16[512,512]{1,0:T(8,128)(2,1)} %param.9) | copy-start | bytes 1572868
  6.5 206.2 %reduce-scatter.4.cloned.1.call-start = ((), (), s32[]{:S(2)}) async-start(), calls=%async_computation.2 | async-start | bytes 6963200
  88.1 15.7 %copy-start.9 = (s32[16]{0:T(128)S(1)}, s32[16]{0:T(128)}, u32[]{:S(2)}) copy-start(s32[16]{0:T(128)} %param.12) | copy-start | bytes 196
  89.2 16.9 %collective-permute-start = (bf16[2,1024,128]{2,1,0:T(8,128)(2,1)S(1)}, bf16[2,1024,128]{2,1,0:T(8,128)(2,1)S(1)}, u32[]{:S(2)}, u32[]{:S(2)}) collective-permute-start(bf16[2,1024,128]{2,1,0:T(8,128)(2,1)S(1)} %copy-done.1), channel_id=1, source_target_pairs={{0,16},{16,0},{32,48},{48,32},{64,80},{80,64},{96,112},{112,96},{1... | collective-permute-start | bytes 1572872 | tf_op jit(solution)/shard_map/ppermute | solution.py:22
  107.5 10.8 %collective-permute-start.1 = (bf16[1024,256]{1,0:T(8,128)(2,1)}, bf16[1024,256]{1,0:T(8,128)(2,1)}, u32[]{:S(2)}, u32[]{:S(2)}) collective-permute-start(bf16[1024,256]{1,0:T(8,128)(2,1)} %get-tuple-element.98), channel_id=1, source_target_pairs={{0,1},{1,0},{2,3},{3,2},{4,5},{5,4},{6,7},{7,6},{8,9},{9,8},{10,11... | collective-permute-start | bytes 1572872 | tf_op jit(solution)/shard_map/ppermute | solution.py:156
  107.5 15.1 %collective-permute-start.2 = (bf16[1024,256]{1,0:T(8,128)(2,1)}, bf16[1024,256]{1,0:T(8,128)(2,1)}, u32[]{:S(2)}, u32[]{:S(2)}) collective-permute-start(bf16[1024,256]{1,0:T(8,128)(2,1)} %get-tuple-element.99), channel_id=1, source_target_pairs={{0,4},{1,5},{2,6},{3,7},{4,0},{5,1},{6,2},{7,3},{8,12},{9,13},{10,... | collective-permute-start | bytes 1572872 | tf_op jit(solution)/shard_map/ppermute | solution.py:156
  109.8 27.3 %collective-permute-start.3 = (bf16[1024,256]{1,0:T(8,128)(2,1)}, bf16[1024,256]{1,0:T(8,128)(2,1)}, u32[]{:S(2)}, u32[]{:S(2)}) collective-permute-start(bf16[1024,256]{1,0:T(8,128)(2,1)} %get-tuple-element.100), channel_id=1, source_target_pairs={{0,5},{1,4},{2,7},{3,6},{4,1},{5,0},{6,3},{7,2},{8,13},{9,12},{10,... | collective-permute-start | bytes 1572872 | tf_op jit(solution)/shard_map/ppermute | solution.py:156
  114.9 38.1 %collective-permute-start.4 = (bf16[1024,256]{1,0:T(8,128)(2,1)S(1)}, bf16[1024,256]{1,0:T(8,128)(2,1)S(1)}, u32[]{:S(2)}, u32[]{:S(2)}) collective-permute-start(bf16[1024,256]{1,0:T(8,128)(2,1)S(1)} %get-tuple-element.101), channel_id=1, source_target_pairs={{0,8},{1,9},{2,10},{3,11},{4,12},{5,13},{6,14},{7,15},{8,0},{9,1},... | collective-permute-start | bytes 1572872 | tf_op jit(solution)/shard_map/ppermute | solution.py:156
  118.2 46.2 %collective-permute-start.5 = (bf16[1024,256]{1,0:T(8,128)(2,1)S(1)}, bf16[1024,256]{1,0:T(8,128)(2,1)S(1)}, u32[]{:S(2)}, u32[]{:S(2)}) collective-permute-start(bf16[1024,256]{1,0:T(8,128)(2,1)S(1)} %get-tuple-element.102), channel_id=1, source_target_pairs={{0,9},{1,8},{2,11},{3,10},{4,13},{5,12},{6,15},{7,14},{8,1},{9,0},... | collective-permute-start | bytes 1572872 | tf_op jit(solution)/shard_map/ppermute | solution.py:156
  118.4 46.0 %collective-permute-start.6 = (bf16[1024,256]{1,0:T(8,128)(2,1)S(1)}, bf16[1024,256]{1,0:T(8,128)(2,1)S(1)}, u32[]{:S(2)}, u32[]{:S(2)}) collective-permute-start(bf16[1024,256]{1,0:T(8,128)(2,1)S(1)} %fusion.43), channel_id=1, source_target_pairs={{0,12},{1,13},{2,14},{3,15},{4,8},{5,9},{6,10},{7,11},{8,4},{9,5},... | collective-permute-start | bytes 1572872 | tf_op jit(solution)/shard_map/ppermute | solution.py:156
  122.7 56.8 %collective-permute-start.7 = (bf16[1024,256]{1,0:T(8,128)(2,1)S(1)}, bf16[1024,256]{1,0:T(8,128)(2,1)S(1)}, u32[]{:S(2)}, u32[]{:S(2)}) collective-permute-start(bf16[1024,256]{1,0:T(8,128)(2,1)S(1)} %get-tuple-element.97), channel_id=1, source_target_pairs={{0,13},{1,12},{2,15},{3,14},{4,9},{5,8},{6,11},{7,10},{8,5},{9,4},... | collective-permute-start | bytes 1572872 | tf_op jit(solution)/shard_map/ppermute | solution.py:156
  221.3 21.3 %copy-start.2 = (bf16[160,128]{0,1:T(8,128)(2,1)}, bf16[160,128]{0,1:T(8,128)(2,1)S(1)}, u32[]{:S(2)}) copy-start(bf16[160,128]{0,1:T(8,128)(2,1)S(1)} %fusion.52) | copy-start | bytes 122884
  221.3 6.7 %collective-permute-start.13 = (bf16[160,1,128]{0,2,1:T(8,128)(2,1)S(1)}, bf16[160,1,128]{0,2,1:T(8,128)(2,1)S(1)}, u32[]{:S(2)}, u32[]{:S(2)}) collective-permute-start(bf16[160,1,128]{0,2,1:T(8,128)(2,1)S(1)} %bitcast.115), channel_id=1, source_target_pairs={{0,16},{16,0},{32,48},{48,32},{64,80},{80,64},{96,112},{112,96},{1... | collective-permute-start | bytes 122888 | tf_op jit(solution)/shard_map/ppermute | solution.py:22
  224.9 17.6 %collective-permute-start.8 = (bf16[160,4,128]{2,0,1:T(8,128)(2,1)S(1)}, bf16[160,4,128]{2,0,1:T(8,128)(2,1)S(1)}, u32[]{:S(2)}, u32[]{:S(2)}) collective-permute-start(bf16[160,4,128]{2,0,1:T(8,128)(2,1)S(1)} %pad_maximum_fusion.1), channel_id=1, source_target_pairs={{0,18},{1,19},{2,16},{3,17},{4,22},{5,23},{6,20},{7,21},{8,26},{9,... | collective-permute-start | bytes 491528 | tf_op jit(solution)/shard_map/ppermute | solution.py:166
  225.0 17.5 %collective-permute-start.9 = (bf16[160,4,128]{2,0,1:T(8,128)(2,1)S(1)}, bf16[160,4,128]{2,0,1:T(8,128)(2,1)S(1)}, u32[]{:S(2)}, u32[]{:S(2)}) collective-permute-start(bf16[160,4,128]{2,0,1:T(8,128)(2,1)S(1)} %pad_maximum_fusion.1), channel_id=1, source_target_pairs={{16,18},{17,19},{18,16},{19,17},{20,22},{21,23},{22,20},{23,21},{2... | collective-permute-start | bytes 491528 | tf_op jit(solution)/shard_map/ppermute | solution.py:167
  242.5 78.2 %copy-start.3 = (bf16[160,128]{0,1:T(8,128)(2,1)S(1)}, bf16[160,128]{0,1:T(8,128)(2,1)}, u32[]{:S(2)}) copy-start(bf16[160,128]{0,1:T(8,128)(2,1)} %copy-done.2) | copy-start | bytes 122884
  242.5 78.2 %copy-start.10 = (f32[160]{0:T(256)S(1)}, f32[160]{0:T(256)}, u32[]{:S(2)}) copy-start(f32[160]{0:T(256)} %fusion.66) | copy-start | bytes 1924
  297.6 23.2 %collective-permute-start.10 = (f32[4,160,128]{2,1,0:T(8,128)S(1)}, f32[4,160,128]{2,1,0:T(8,128)S(1)}, u32[]{:S(2)}, u32[]{:S(2)}) collective-permute-start(f32[4,160,128]{2,1,0:T(8,128)S(1)} %get-tuple-element.107), channel_id=1, source_target_pairs={{16,18},{17,19},{18,16},{19,17},{20,22},{21,23},{22,20},{23,21},{2... | collective-permute-start | bytes 983048 | tf_op jit(solution)/shard_map/ppermute | solution.py:183
  301.4 19.4 %collective-permute-start.14 = (f32[4,160,128]{2,1,0:T(8,128)S(1)}, f32[4,160,128]{2,1,0:T(8,128)S(1)}, u32[]{:S(2)}, u32[]{:S(2)}) collective-permute-start(f32[4,160,128]{2,1,0:T(8,128)S(1)} %get-tuple-element.108), channel_id=1, source_target_pairs={{0,16},{1,17},{2,18},{3,19},{4,20},{5,21},{6,22},{7,23},{8,24},{9,... | collective-permute-start | bytes 983048 | tf_op jit(solution)/shard_map/ppermute | solution.py:182
  301.5 15.6 %collective-permute-start.11 = (f32[4,160]{1,0:T(4,128)S(1)}, f32[4,160]{1,0:T(4,128)S(1)}, u32[]{:S(2)}, u32[]{:S(2)}) collective-permute-start(f32[4,160]{1,0:T(4,128)S(1)} %get-tuple-element.115), channel_id=1, source_target_pairs={{16,18},{17,19},{18,16},{19,17},{20,22},{21,23},{22,20},{23,21},{2... | collective-permute-start | bytes 7688 | tf_op jit(solution)/shard_map/ppermute | solution.py:183
  307.5 10.9 %collective-permute-start.12 = (f32[4,160]{1,0:T(4,128)S(1)}, f32[4,160]{1,0:T(4,128)S(1)}, u32[]{:S(2)}, u32[]{:S(2)}) collective-permute-start(f32[4,160]{1,0:T(4,128)S(1)} %get-tuple-element.116), channel_id=1, source_target_pairs={{0,16},{1,17},{2,18},{3,19},{4,20},{5,21},{6,22},{7,23},{8,24},{9,... | collective-permute-start | bytes 7688 | tf_op jit(solution)/shard_map/ppermute | solution.py:182
  307.6 10.8 %collective-permute-start.15 = (f32[4,160]{1,0:T(4,128)S(1)}, f32[4,160]{1,0:T(4,128)S(1)}, u32[]{:S(2)}, u32[]{:S(2)}) collective-permute-start(f32[4,160]{1,0:T(4,128)S(1)} %get-tuple-element.117), channel_id=1, source_target_pairs={{16,18},{17,19},{18,16},{19,17},{20,22},{21,23},{22,20},{23,21},{2... | collective-permute-start | bytes 7688 | tf_op jit(solution)/shard_map/ppermute | solution.py:183
  317.1 3.6 %collective-permute-start.16 = (f32[4,160]{1,0:T(4,128)S(1)}, f32[4,160]{1,0:T(4,128)S(1)}, u32[]{:S(2)}, u32[]{:S(2)}) collective-permute-start(f32[4,160]{1,0:T(4,128)S(1)} %get-tuple-element.118), channel_id=1, source_target_pairs={{0,16},{1,17},{2,18},{3,19},{4,20},{5,21},{6,22},{7,23},{8,24},{9,... | collective-permute-start | bytes 7688 | tf_op jit(solution)/shard_map/ppermute | solution.py:182
  (8 other events, 36.9 us)
Sparse Core Ops, SparseCore 0:
  88.3 124.3 reduce-scatter.3
